TPU v7x, 256 devices: a whole 4x4x8 slice. The times are simulated.
256 devices in a mesh: dp: 2 (over core), ctx: 8 (over y, z_lo), feat: 16 (over x, z_hi).
Axes of the slice: x: 4, y: 4, z: 8 (z_hi: 4, z_lo: 2; z = z_hi * 2 + z_lo), core: 2. Of those that a mesh axis runs over, the one named last changes fastest.
Arguments:
- out_grads: bfloat16 [2048, 28672], P(('dp', 'ctx'), 'feat'), may hold values from -6 to 6
- acts: bfloat16 [2048, 8192], P(('dp', 'ctx'), 'feat'), may hold values from -6 to 6
- domain_ids: int32 [2048], P(('dp', 'ctx')), may hold values from 0 to 7
- domain_weights: int32 [8], replicated, may hold values from 1 to 4
Outputs:
- grad_factor: bfloat16 [28672, 28672], P(('dp', 'ctx'), 'feat')
- act_factor: bfloat16 [8192, 8192], P(('dp', 'ctx'), 'feat')
All inputs are finite; a program needn't handle non-finite values.
Results may differ from a plain program's by a relative error of at most 0.003.
Values may be sent and summed in bfloat16 or wider, within the bound.
No kernel may reach another device: no remote copies, remote signals or barrier semaphores. Data moves between devices by JAX's collectives and lax.ppermute only.
A program may use at most 128 MiB of HBM per device.

v0:
```python
import jax
import jax.numpy as jnp
from jax import lax
from jax.sharding import PartitionSpec as P

ROWS = ("dp", "ctx")
PAIR = 2


def token_weights(tok_ids, domain_weights):
    labels = jnp.arange(domain_weights.shape[0], dtype=jnp.int32)
    match = tok_ids[:, None] == labels[None, :]
    return jnp.sum(jnp.where(match, domain_weights[None, :], 0), axis=1).astype(jnp.float32)


def contract_tokens(left, right):
    return lax.dot_general(
        left, right, (((0,), (0,)), ((), ())), preferred_element_type=jnp.float32
    )


def split_row(r, n_ring):
    per_dp = n_ring * PAIR
    return (r // per_dp, r % per_dp // PAIR, r % PAIR)


def token_block(r, p, n_dp, n_ring):
    dp, y, z = split_row(r, n_ring)
    ddp, dy, dz = split_row(p, n_ring)
    return (dp + ddp) % n_dp * n_ring * PAIR + (y + dy) % n_ring * PAIR + (z + dz) % PAIR


def transpose_pairs(n_rows, n_cols, n_dp, n_ring):
    return [
        (token_block(r, c, n_dp, n_ring) * n_cols + r, r * n_cols + c)
        for r in range(n_rows)
        for c in range(n_cols)
    ]


def ctx_shift(n_ring, dy, dz):
    pairs = []
    for y in range(n_ring):
        for z in range(PAIR):
            src = (y + dy) % n_ring * PAIR + (z + dz) % PAIR
            pairs.append((src, y * PAIR + z))
    return pairs


def gather_columns(block, n_dp, n_ring):
    half = block.shape[0]
    near = lax.ppermute(block, "ctx", ctx_shift(n_ring, 0, 1))
    own = jnp.concatenate([block, near], axis=0)
    ahead = lax.ppermute(own, "ctx", ctx_shift(n_ring, 1, 0))
    behind = lax.ppermute(own, "ctx", ctx_shift(n_ring, -1, 0))
    far_a = lax.ppermute(ahead[:half], "ctx", ctx_shift(n_ring, 1, 0))
    far_b = lax.ppermute(behind[half:], "ctx", ctx_shift(n_ring, -1, 0))
    mine = jnp.concatenate([own, ahead, far_a, far_b, behind], axis=0)
    other = lax.ppermute(mine, "dp", [(1, 0), (0, 1)])
    return jnp.concatenate([mine, other], axis=0)


def local(out_grads, acts, domain_ids, domain_weights):
    n_dp = lax.axis_size("dp")
    n_ctx = lax.axis_size("ctx")
    n_rows = n_dp * n_ctx
    n_cols = lax.axis_size("feat")
    n_ring = n_ctx // PAIR
    assert n_rows == n_cols and n_dp == 2 and (n_ring == 4) and (n_ctx % PAIR == 0)
    inv_count = 1.0 / (out_grads.shape[0] * n_rows)
    width_g = out_grads.shape[1]
    both = jnp.concatenate([out_grads, acts], axis=1)
    tok_weight = token_weights(domain_ids, domain_weights)
    weighted = (tok_weight[:, None] * both.astype(jnp.float32)).astype(jnp.bfloat16)
    pairs = transpose_pairs(n_rows, n_cols, n_dp, n_ring)
    swapped = jnp.concatenate(
        [
            lax.ppermute(out_grads, ROWS + ("feat",), pairs),
            lax.ppermute(acts, ROWS + ("feat",), pairs),
        ],
        axis=1,
    )
    rows = lax.all_gather(swapped, "feat", axis=0, tiled=True)
    cols = gather_columns(weighted, n_dp, n_ring)
    grad_sum = contract_tokens(rows[:, :width_g], cols[:, :width_g])
    act_sum = contract_tokens(rows[:, width_g:], lax.optimization_barrier(cols[:, width_g:]))
    grad_factor = (grad_sum * inv_count).astype(jnp.bfloat16)
    act_factor = (act_sum * inv_count).astype(jnp.bfloat16)
    return (grad_factor, act_factor)


def solution(mesh):
    in_specs = (P(ROWS, "feat"), P(ROWS, "feat"), P(ROWS), P())
    out_specs = (P(ROWS, "feat"), P(ROWS, "feat"))
    return jax.shard_map(local, mesh=mesh, in_specs=in_specs, out_specs=out_specs, check_vma=False)
```

profile of v0, /device:TPU:34, one launch (start us, length us, event | category | flops | bytes accessed | tf_op | source)
XLA Modules:
  0.0 204.5 jit_solution(8906525784769521334)
XLA Ops:
  7.2 0.0 all-gather.2.cloned.1.call-start
  7.2 6.5 %collective-permute-start = (bf16[128,1792]{1,0:T(8,128)(2,1)}, bf16[128,1792]{1,0:T(8,128)(2,1)S(1)}, u32[]{:S(2)}, u32[]{:S(2)}) collective-permute-start(bf16[128,1792]{1,0:T(8,128)(2,1)} %param.4), channel_id=1, source_target_pairs={{0,0},{16,1},{32,2},{48,3},{64,4},{80,5},{96,6},{112,7},{128,8},{1... | collective-permute-start | bytes 1376264 | tf_op jit(solution)/shard_map/ppermute | solution.py:78
  13.7 3.8 %collective-permute-start.1 = (bf16[128,512]{1,0:T(8,128)(2,1)}, bf16[128,512]{1,0:T(8,128)(2,1)S(1)}, u32[]{:S(2)}, u32[]{:S(2)}) collective-permute-start(bf16[128,512]{1,0:T(8,128)(2,1)} %param.5), channel_id=1, source_target_pairs={{0,0},{16,1},{32,2},{48,3},{64,4},{80,5},{96,6},{112,7},{128,8},{1... | collective-permute-start | bytes 393224 | tf_op jit(solution)/shard_map/ppermute | solution.py:79
  17.5 12.0 %collective-permute-done.1 = bf16[128,512]{1,0:T(8,128)(2,1)S(1)} collective-permute-done((bf16[128,512]{1,0:T(8,128)(2,1)}, bf16[128,512]{1,0:T(8,128)(2,1)S(1)}, u32[]{:S(2)}, u32[]{:S(2)}) %collective-permute-start.1) | collective-permute-done | bytes 131104 | tf_op jit(solution)/shard_map/ppermute | solution.py:79
  29.5 0.9 pad_maximum_fusion.1
  30.3 0.0 all-gather.2.cloned.1.call-update
  30.4 0.8 select_reduce_fusion
  31.1 1.3 constant_dynamic-update-slice_fusion.5
  32.4 0.1 collective-permute-start.2
  32.5 14.8 %collective-permute-done.2 = bf16[128,2304]{1,0:T(8,128)(2,1)S(1)} collective-permute-done((bf16[128,2304]{1,0:T(8,128)(2,1)S(1)}, bf16[128,2304]{1,0:T(8,128)(2,1)S(1)}, u32[]{:S(2)}, u32[]{:S(2)}) %collective-permute-start.2) | collective-permute-done | bytes 589856 | tf_op jit(solution)/shard_map/ppermute | solution.py:52
  47.3 0.1 pad_maximum_fusion
  47.4 15.8 %collective-permute-start.3 = (bf16[256,2304]{1,0:T(8,128)(2,1)S(1)}, bf16[256,2304]{1,0:T(8,128)(2,1)S(1)}, u32[]{:S(2)}, u32[]{:S(2)}) collective-permute-start(bf16[256,2304]{1,0:T(8,128)(2,1)S(1)} %pad_maximum_fusion), channel_id=1, source_target_pairs={{32,0},{48,16},{64,32},{80,48},{96,64},{112,80},{0,96},{16,112},{3... | collective-permute-start | bytes 3538952 | tf_op jit(solution)/shard_map/ppermute | solution.py:54
  63.2 1.0 collective-permute-start.5
  64.2 23.6 %collective-permute-done.3 = bf16[256,2304]{1,0:T(8,128)(2,1)S(1)} collective-permute-done((bf16[256,2304]{1,0:T(8,128)(2,1)S(1)}, bf16[256,2304]{1,0:T(8,128)(2,1)S(1)}, u32[]{:S(2)}, u32[]{:S(2)}) %collective-permute-start.3) | collective-permute-done | bytes 1179680 | tf_op jit(solution)/shard_map/ppermute | solution.py:54
  87.8 3.7 %collective-permute-start.4 = (bf16[128,2304]{1,0:T(8,128)(2,1)S(1)}, bf16[128,2304]{1,0:T(8,128)(2,1)S(1)}, u32[]{:S(2)}, u32[]{:S(2)}) collective-permute-start(bf16[128,2304]{1,0:T(8,128)(2,1)S(1)} %slice.25), channel_id=1, source_target_pairs={{32,0},{48,16},{64,32},{80,48},{96,64},{112,80},{0,96},{16,112},{3... | collective-permute-start | bytes 1769480 | tf_op jit(solution)/shard_map/ppermute | solution.py:56
  91.5 0.1 constant_dynamic-update-slice_fusion.4
  91.6 0.1 collective-permute-done.5
  91.7 0.6 collective-permute-start.6
  92.4 0.2 constant_dynamic-update-slice_fusion.3
  92.5 12.1 %collective-permute-done.4 = bf16[128,2304]{1,0:T(8,128)(2,1)S(1)} collective-permute-done((bf16[128,2304]{1,0:T(8,128)(2,1)S(1)}, bf16[128,2304]{1,0:T(8,128)(2,1)S(1)}, u32[]{:S(2)}, u32[]{:S(2)}) %collective-permute-start.4) | collective-permute-done | bytes 589856 | tf_op jit(solution)/shard_map/ppermute | solution.py:56
  104.6 0.1 constant_dynamic-update-slice_fusion.2
  104.7 4.2 %collective-permute-done.6 = bf16[128,2304]{1,0:T(8,128)(2,1)S(1)} collective-permute-done((bf16[128,2304]{1,0:T(8,128)(2,1)S(1)}, bf16[128,2304]{1,0:T(8,128)(2,1)S(1)}, u32[]{:S(2)}, u32[]{:S(2)}) %collective-permute-start.6) | collective-permute-done | bytes 589856 | tf_op jit(solution)/shard_map/ppermute | solution.py:57
  108.9 0.1 constant_dynamic-update-slice_fusion.1
  109.0 0.2 constant_dynamic-update-slice_fusion
  109.2 0.8 collective-permute-start.7
  110.0 7.5 %collective-permute-done.7 = bf16[1024,2304]{1,0:T(8,128)(2,1)S(1)} collective-permute-done((bf16[1024,2304]{1,0:T(8,128)(2,1)S(1)}, bf16[1024,2304]{1,0:T(8,128)(2,1)S(1)}, u32[]{:S(2)}, u32[]{:S(2)}) %collective-permute-start.7) | collective-permute-done | bytes 4718624 | tf_op jit(solution)/shard_map/ppermute | solution.py:59
  117.5 0.3 constant_dynamic-update-slice_fusion.6
  117.8 3.6 %copy-done = bf16[2048,2304]{1,0:T(8,128)(2,1)} copy-done((bf16[2048,2304]{1,0:T(8,128)(2,1)}, bf16[2048,2304]{1,0:T(8,128)(2,1)S(1)}, u32[]{:S(2)}) %copy-start) | copy-done | bytes 9437208
  121.5 0.2 slice.29
  121.6 52.6 %all-gather.2.cloned.1.call-done = bf16[2048,2304]{1,0:T(8,128)(2,1)} async-done(((bf16[128,2304]{1,0:T(8,128)(2,1)}), bf16[2048,2304]{1,0:T(8,128)(2,1)}) %all-gather.2.cloned.1.call-update) | async-done | bytes 9437200 | tf_op jit(solution)/shard_map/all_gather | solution.py:83
  174.2 19.8 %multiply_convert_fusion = bf16[1792,1792]{1,0:T(8,128)(2,1)} fusion(bf16[2048,2304]{1,0:T(8,128)(2,1)} %copy-done, bf16[2048,2304]{1,0:T(8,128)(2,1)} %all-gather.2.cloned.1.call-done), kind=kOutput, calls=%fused_computation | convolution fusion | flops 13159759872 | bytes 21102592 | tf_op jit(solution)/shard_map/dot_general | solution.py:17
  194.0 3.7 %fusion.7 = bf16[512,512]{1,0:T(8,128)(2,1)} fusion(bf16[2048,512]{1,0:T(8,128)(2,1)S(1)} %slice.29, bf16[2048,2304]{1,0:T(8,128)(2,1)} %all-gather.2.cloned.1.call-done), kind=kOutput, calls=%fused_computation.6 | convolution fusion | flops 1074266112 | bytes 4718592 | tf_op jit(solution)/shard_map/dot_general | solution.py:17
  (6 shorter events, 0.1 us)
Async XLA Ops:
  7.2 167.1 %all-gather.2.cloned.1.call-start = ((), (), s32[]{:S(2)}) async-start(), calls=%async_computation | async-start | bytes 10027008 | tf_op jit(solution)/shard_map/all_gather | solution.py:83
  7.2 22.3 %collective-permute-start = (bf16[128,1792]{1,0:T(8,128)(2,1)}, bf16[128,1792]{1,0:T(8,128)(2,1)S(1)}, u32[]{:S(2)}, u32[]{:S(2)}) collective-permute-start(bf16[128,1792]{1,0:T(8,128)(2,1)} %param.4), channel_id=1, source_target_pairs={{0,0},{16,1},{32,2},{48,3},{64,4},{80,5},{96,6},{112,7},{128,8},{1... | collective-permute-start | bytes 1376264 | tf_op jit(solution)/shard_map/ppermute | solution.py:78
  13.7 15.8 %collective-permute-start.1 = (bf16[128,512]{1,0:T(8,128)(2,1)}, bf16[128,512]{1,0:T(8,128)(2,1)S(1)}, u32[]{:S(2)}, u32[]{:S(2)}) collective-permute-start(bf16[128,512]{1,0:T(8,128)(2,1)} %param.5), channel_id=1, source_target_pairs={{0,0},{16,1},{32,2},{48,3},{64,4},{80,5},{96,6},{112,7},{128,8},{1... | collective-permute-start | bytes 393224 | tf_op jit(solution)/shard_map/ppermute | solution.py:79
  32.4 14.9 %collective-permute-start.2 = (bf16[128,2304]{1,0:T(8,128)(2,1)S(1)}, bf16[128,2304]{1,0:T(8,128)(2,1)S(1)}, u32[]{:S(2)}, u32[]{:S(2)}) collective-permute-start(bf16[128,2304]{1,0:T(8,128)(2,1)S(1)} %get-tuple-element.3), channel_id=1, source_target_pairs={{16,0},{0,16},{48,32},{32,48},{80,64},{64,80},{112,96},{96,112},{1... | collective-permute-start | bytes 1769480 | tf_op jit(solution)/shard_map/ppermute | solution.py:52
  47.4 40.4 %collective-permute-start.3 = (bf16[256,2304]{1,0:T(8,128)(2,1)S(1)}, bf16[256,2304]{1,0:T(8,128)(2,1)S(1)}, u32[]{:S(2)}, u32[]{:S(2)}) collective-permute-start(bf16[256,2304]{1,0:T(8,128)(2,1)S(1)} %pad_maximum_fusion), channel_id=1, source_target_pairs={{32,0},{48,16},{64,32},{80,48},{96,64},{112,80},{0,96},{16,112},{3... | collective-permute-start | bytes 3538952 | tf_op jit(solution)/shard_map/ppermute | solution.py:54
  63.2 28.5 %collective-permute-start.5 = (bf16[256,2304]{1,0:T(8,128)(2,1)S(1)}, bf16[256,2304]{1,0:T(8,128)(2,1)S(1)}, u32[]{:S(2)}, u32[]{:S(2)}) collective-permute-start(bf16[256,2304]{1,0:T(8,128)(2,1)S(1)} %pad_maximum_fusion), channel_id=1, source_target_pairs={{96,0},{112,16},{0,32},{16,48},{32,64},{48,80},{64,96},{80,112},{9... | collective-permute-start | bytes 3538952 | tf_op jit(solution)/shard_map/ppermute | solution.py:55
  87.8 16.8 %collective-permute-start.4 = (bf16[128,2304]{1,0:T(8,128)(2,1)S(1)}, bf16[128,2304]{1,0:T(8,128)(2,1)S(1)}, u32[]{:S(2)}, u32[]{:S(2)}) collective-permute-start(bf16[128,2304]{1,0:T(8,128)(2,1)S(1)} %slice.25), channel_id=1, source_target_pairs={{32,0},{48,16},{64,32},{80,48},{96,64},{112,80},{0,96},{16,112},{3... | collective-permute-start | bytes 1769480 | tf_op jit(solution)/shard_map/ppermute | solution.py:56
  91.7 17.2 %collective-permute-start.6 = (bf16[128,2304]{1,0:T(8,128)(2,1)S(1)}, bf16[128,2304]{1,0:T(8,128)(2,1)S(1)}, u32[]{:S(2)}, u32[]{:S(2)}) collective-permute-start(bf16[128,2304]{1,0:T(8,128)(2,1)S(1)} %slice.26), channel_id=1, source_target_pairs={{96,0},{112,16},{0,32},{16,48},{32,64},{48,80},{64,96},{80,112},{9... | collective-permute-start | bytes 1769480 | tf_op jit(solution)/shard_map/ppermute | solution.py:57
  109.2 8.3 %collective-permute-start.7 = (bf16[1024,2304]{1,0:T(8,128)(2,1)S(1)}, bf16[1024,2304]{1,0:T(8,128)(2,1)S(1)}, u32[]{:S(2)}, u32[]{:S(2)}) collective-permute-start(bf16[1024,2304]{1,0:T(8,128)(2,1)S(1)} %get-tuple-element.4), channel_id=1, source_target_pairs={{128,0},{0,128},{129,1},{1,129},{130,2},{2,130},{131,3},{3,131},{1... | collective-permute-start | bytes 14155784 | tf_op jit(solution)/shard_map/ppermute | solution.py:59
  117.8 3.7 %copy-start = (bf16[2048,2304]{1,0:T(8,128)(2,1)}, bf16[2048,2304]{1,0:T(8,128)(2,1)S(1)}, u32[]{:S(2)}) copy-start(bf16[2048,2304]{1,0:T(8,128)(2,1)S(1)} %constant_dynamic-update-slice_fusion.6) | copy-start | bytes 28311556
Sparse Core Ops, SparseCore 0:
  30.5 143.6 all-gather.1
where the time goes:
time: 205 us
  waiting for transfers between devices  127 us (62%)
  starting transfers between devices  32.2 us (16%)
  matrix products  23.5 us (11%)
  between operations  14.1 us (7%)
  local copies, waits for them, and re-layouts  4.76 us (2%)
  other arithmetic  2.95 us (1%)
    all_gather x1, waiting for transfers between devices, local(): rows = lax.all_gather(swapped, 'feat', axis=0, tiled=True)  52.6 us
    ppermute x1, waiting for transfers between devices, gather_columns(): ahead = lax.ppermute(own, 'ctx', ctx_shift(n_ring, 1, 0))  23.6 us
    dot_general x2, matrix products, contract_tokens(): lax.dot_general(left, right, (((0,), (0,)), ((), ())), preferred_element_...  23.5 us
    ppermute x1, starting transfers between devices, gather_columns(): ahead = lax.ppermute(own, 'ctx', ctx_shift(n_ring, 1, 0))  15.8 us
    ppermute x1, waiting for transfers between devices, gather_columns(): near = lax.ppermute(block, 'ctx', ctx_shift(n_ring, 0, 1))  14.8 us
    ppermute x1, waiting for transfers between devices, gather_columns(): far_a = lax.ppermute(ahead[:half], 'ctx', ctx_shift(n_ring, 1, 0))  12.1 us
    ppermute x1, waiting for transfers between devices, local(): lax.ppermute(acts, ROWS + ('feat',), pairs)  12 us
    ppermute x1, waiting for transfers between devices, gather_columns(): other = lax.ppermute(mine, 'dp', [(1, 0), (0, 1)])  7.54 us
  transfers between devices with their start and end apart: 9, of which 8 were waited for; matrix products, arithmetic and copies ran while one was open for 2% of the time, Pallas kernels for 0%

commit v1 on v0

--- a/solution.py
+++ b/solution.py
@@ -80,7 +80,9 @@
         ],
         axis=1,
     )
-    rows = lax.all_gather(swapped, "feat", axis=0, tiled=True)
+    rows = jnp.concatenate(
+        lax.all_to_all(jnp.stack([swapped] * lax.axis_size("feat")), "feat", 0, 0), axis=0
+    )
     cols = gather_columns(weighted, n_dp, n_ring)
     grad_sum = contract_tokens(rows[:, :width_g], cols[:, :width_g])
     act_sum = contract_tokens(rows[:, width_g:], lax.optimization_barrier(cols[:, width_g:]))

time: 205 us -> 381 us (1.86)
  the two profiles are of different devices: /device:TPU:34 before, /device:TPU:195 now
where the time goes in v1:
time: 381 us
  waiting for transfers between devices  324 us (85%)
  matrix products  23.6 us (6%)
  starting transfers between devices  22.4 us (6%)
  local copies, waits for them, and re-layouts  9.4 us (2%)
    ppermute x1, waiting for transfers between devices, gather_columns(): near = lax.ppermute(block, 'ctx', ctx_shift(n_ring, 0, 1))  250 us
    ppermute x1, waiting for transfers between devices, local(): lax.ppermute(acts, ROWS + ('feat',), pairs)  27 us
    ppermute x1, waiting for transfers between devices, gather_columns(): ahead = lax.ppermute(own, 'ctx', ctx_shift(n_ring, 1, 0))  25.4 us
    dot_general x2, matrix products, contract_tokens(): lax.dot_general(left, right, (((0,), (0,)), ((), ())), preferred_element_...  23.6 us
    ppermute x1, waiting for transfers between devices, gather_columns(): far_a = lax.ppermute(ahead[:half], 'ctx', ctx_shift(n_ring, 1, 0))  11.4 us
  transfers between devices with their start and end apart: 9, of which 6 were waited for; matrix products, arithmetic and copies ran while one was open for 0% of the time, Pallas kernels for 0%

profile of v1, /device:TPU:195, one launch (start us, length us, event | category | flops | bytes accessed | tf_op | source)
XLA Modules:
  0.0 380.8 jit_solution(12577616481432010250)
XLA Ops:
  0.6 6.6 %collective-permute-start = (bf16[128,1792]{1,0:T(8,128)(2,1)}, bf16[128,1792]{1,0:T(8,128)(2,1)S(1)}, u32[]{:S(2)}, u32[]{:S(2)}) collective-permute-start(bf16[128,1792]{1,0:T(8,128)(2,1)} %param.4), channel_id=1, source_target_pairs={{0,0},{16,1},{32,2},{48,3},{64,4},{80,5},{96,6},{112,7},{128,8},{1... | collective-permute-start | bytes 1376264 | tf_op jit(solution)/shard_map/ppermute | solution.py:78
  7.2 1.9 collective-permute-start.1
  9.2 27.0 %collective-permute-done.1 = bf16[128,512]{1,0:T(8,128)(2,1)S(1)} collective-permute-done((bf16[128,512]{1,0:T(8,128)(2,1)}, bf16[128,512]{1,0:T(8,128)(2,1)S(1)}, u32[]{:S(2)}, u32[]{:S(2)}) %collective-permute-start.1) | collective-permute-done | bytes 131104 | tf_op jit(solution)/shard_map/ppermute | solution.py:79
  36.2 0.0 collective-permute-done
  36.2 4.6 %stack.2 = bf16[16,128,2304]{2,1,0:T(8,128)(2,1)} broadcast(bf16[128,2304]{1,0:T(8,128)(2,1)S(1)} %pad_maximum_fusion.1), dimensions={1,2} | broadcast | bytes 10027008 | tf_op jit(solution)/shard_map/stack | solution.py:84
  40.8 7.1 %all-to-all-start = ((bf16[16,128,2304]{2,1,0:T(8,128)(2,1)}), bf16[16,128,2304]{2,1,0:T(8,128)(2,1)}, u32[]{:S(2)}, u32[]{:S(2)}) async-start(bf16[16,128,2304]{2,1,0:T(8,128)(2,1)} %stack.2), calls=%async_computation | async-start | bytes 18874368 | tf_op jit(solution)/shard_map/all_to_all | solution.py:84
  47.9 0.1 select_reduce_fusion
  48.0 0.2 constant_dynamic-update-slice_fusion.5
  48.2 0.9 collective-permute-start.2
  49.1 250.0 %collective-permute-done.2 = bf16[128,2304]{1,0:T(8,128)(2,1)S(1)} collective-permute-done((bf16[128,2304]{1,0:T(8,128)(2,1)S(1)}, bf16[128,2304]{1,0:T(8,128)(2,1)S(1)}, u32[]{:S(2)}, u32[]{:S(2)}) %collective-permute-start.2) | collective-permute-done | bytes 589856 | tf_op jit(solution)/shard_map/ppermute | solution.py:52
  299.2 0.1 pad_maximum_fusion
  299.2 0.1 collective-permute-start.3
  299.3 1.5 collective-permute-start.5
  300.8 25.4 %collective-permute-done.3 = bf16[256,2304]{1,0:T(8,128)(2,1)S(1)} collective-permute-done((bf16[256,2304]{1,0:T(8,128)(2,1)S(1)}, bf16[256,2304]{1,0:T(8,128)(2,1)S(1)}, u32[]{:S(2)}, u32[]{:S(2)}) %collective-permute-start.3) | collective-permute-done | bytes 1179680 | tf_op jit(solution)/shard_map/ppermute | solution.py:54
  326.2 1.6 collective-permute-start.4
  327.9 0.1 constant_dynamic-update-slice_fusion.4
  327.9 0.0 collective-permute-done.5
  328.0 0.1 collective-permute-start.6
  328.1 0.2 constant_dynamic-update-slice_fusion.3
  328.3 11.4 %collective-permute-done.4 = bf16[128,2304]{1,0:T(8,128)(2,1)S(1)} collective-permute-done((bf16[128,2304]{1,0:T(8,128)(2,1)S(1)}, bf16[128,2304]{1,0:T(8,128)(2,1)S(1)}, u32[]{:S(2)}, u32[]{:S(2)}) %collective-permute-start.4) | collective-permute-done | bytes 589856 | tf_op jit(solution)/shard_map/ppermute | solution.py:56
  339.7 0.1 constant_dynamic-update-slice_fusion.2
  339.7 2.9 collective-permute-done.6
  342.7 0.1 constant_dynamic-update-slice_fusion.1
  342.8 0.2 constant_dynamic-update-slice_fusion
  342.9 2.6 collective-permute-start.7
  345.5 7.5 %collective-permute-done.7 = bf16[1024,2304]{1,0:T(8,128)(2,1)S(1)} collective-permute-done((bf16[1024,2304]{1,0:T(8,128)(2,1)S(1)}, bf16[1024,2304]{1,0:T(8,128)(2,1)S(1)}, u32[]{:S(2)}, u32[]{:S(2)}) %collective-permute-start.7) | collective-permute-done | bytes 4718624 | tf_op jit(solution)/shard_map/ppermute | solution.py:59
  353.1 0.3 constant_dynamic-update-slice_fusion.6
  353.4 3.7 copy-done
  357.1 0.2 slice.29
  357.3 0.0 all-to-all-done
  357.3 19.9 %multiply_convert_fusion = bf16[1792,1792]{1,0:T(8,128)(2,1)} fusion(bf16[2048,2304]{1,0:T(8,128)(2,1)} %copy-done, bf16[2048,2304]{1,0:T(8,128)(2,1)} %bitcast), kind=kOutput, calls=%fused_computation | convolution fusion | flops 13159759872 | bytes 21102592 | tf_op jit(solution)/shard_map/dot_general | solution.py:17
  377.2 3.7 fusion.7
  (14 shorter events, 0.2 us)
Async XLA Ops:
  0.6 35.5 %collective-permute-start = (bf16[128,1792]{1,0:T(8,128)(2,1)}, bf16[128,1792]{1,0:T(8,128)(2,1)S(1)}, u32[]{:S(2)}, u32[]{:S(2)}) collective-permute-start(bf16[128,1792]{1,0:T(8,128)(2,1)} %param.4), channel_id=1, source_target_pairs={{0,0},{16,1},{32,2},{48,3},{64,4},{80,5},{96,6},{112,7},{128,8},{1... | collective-permute-start | bytes 1376264 | tf_op jit(solution)/shard_map/ppermute | solution.py:78
  7.2 28.9 %collective-permute-start.1 = (bf16[128,512]{1,0:T(8,128)(2,1)}, bf16[128,512]{1,0:T(8,128)(2,1)S(1)}, u32[]{:S(2)}, u32[]{:S(2)}) collective-permute-start(bf16[128,512]{1,0:T(8,128)(2,1)} %param.5), channel_id=1, source_target_pairs={{0,0},{16,1},{32,2},{48,3},{64,4},{80,5},{96,6},{112,7},{128,8},{1... | collective-permute-start | bytes 393224 | tf_op jit(solution)/shard_map/ppermute | solution.py:79
  40.8 7.1 %copy-start.3 = (s32[8]{0:T(128)S(1)}, s32[8]{0:T(128)}, u32[]{:S(2)}) copy-start(s32[8]{0:T(128)} %param.7) | copy-start | bytes 100
  40.8 7.1 %copy-start.4 = (s32[128]{0:T(128)S(1)}, s32[128]{0:T(128)}, u32[]{:S(2)}) copy-start(s32[128]{0:T(128)} %param.6) | copy-start | bytes 1540
  40.8 7.2 %copy-start.1 = (bf16[128,1792]{1,0:T(8,128)(2,1)S(1)}, bf16[128,1792]{1,0:T(8,128)(2,1)}, u32[]{:S(2)}) copy-start(bf16[128,1792]{1,0:T(8,128)(2,1)} %param.4) | copy-start | bytes 1376260
  40.8 7.2 %copy-start.2 = (bf16[128,512]{1,0:T(8,128)(2,1)S(1)}, bf16[128,512]{1,0:T(8,128)(2,1)}, u32[]{:S(2)}) copy-start(bf16[128,512]{1,0:T(8,128)(2,1)} %param.5) | copy-start | bytes 393220
  40.8 316.5 %all-to-all-start = ((bf16[16,128,2304]{2,1,0:T(8,128)(2,1)}), bf16[16,128,2304]{2,1,0:T(8,128)(2,1)}, u32[]{:S(2)}, u32[]{:S(2)}) async-start(bf16[16,128,2304]{2,1,0:T(8,128)(2,1)} %stack.2), calls=%async_computation | async-start | bytes 18874368 | tf_op jit(solution)/shard_map/all_to_all | solution.py:84
  48.2 251.0 %collective-permute-start.2 = (bf16[128,2304]{1,0:T(8,128)(2,1)S(1)}, bf16[128,2304]{1,0:T(8,128)(2,1)S(1)}, u32[]{:S(2)}, u32[]{:S(2)}) collective-permute-start(bf16[128,2304]{1,0:T(8,128)(2,1)S(1)} %get-tuple-element.3), channel_id=1, source_target_pairs={{16,0},{0,16},{48,32},{32,48},{80,64},{64,80},{112,96},{96,112},{1... | collective-permute-start | bytes 1769480 | tf_op jit(solution)/shard_map/ppermute | solution.py:52
  299.2 27.0 %collective-permute-start.3 = (bf16[256,2304]{1,0:T(8,128)(2,1)S(1)}, bf16[256,2304]{1,0:T(8,128)(2,1)S(1)}, u32[]{:S(2)}, u32[]{:S(2)}) collective-permute-start(bf16[256,2304]{1,0:T(8,128)(2,1)S(1)} %pad_maximum_fusion), channel_id=1, source_target_pairs={{32,0},{48,16},{64,32},{80,48},{96,64},{112,80},{0,96},{16,112},{3... | collective-permute-start | bytes 3538952 | tf_op jit(solution)/shard_map/ppermute | solution.py:54
  299.3 28.6 %collective-permute-start.5 = (bf16[256,2304]{1,0:T(8,128)(2,1)S(1)}, bf16[256,2304]{1,0:T(8,128)(2,1)S(1)}, u32[]{:S(2)}, u32[]{:S(2)}) collective-permute-start(bf16[256,2304]{1,0:T(8,128)(2,1)S(1)} %pad_maximum_fusion), channel_id=1, source_target_pairs={{96,0},{112,16},{0,32},{16,48},{32,64},{48,80},{64,96},{80,112},{9... | collective-permute-start | bytes 3538952 | tf_op jit(solution)/shard_map/ppermute | solution.py:55
  326.2 13.4 %collective-permute-start.4 = (bf16[128,2304]{1,0:T(8,128)(2,1)S(1)}, bf16[128,2304]{1,0:T(8,128)(2,1)S(1)}, u32[]{:S(2)}, u32[]{:S(2)}) collective-permute-start(bf16[128,2304]{1,0:T(8,128)(2,1)S(1)} %slice.25), channel_id=1, source_target_pairs={{32,0},{48,16},{64,32},{80,48},{96,64},{112,80},{0,96},{16,112},{3... | collective-permute-start | bytes 1769480 | tf_op jit(solution)/shard_map/ppermute | solution.py:56
  328.0 14.7 %collective-permute-start.6 = (bf16[128,2304]{1,0:T(8,128)(2,1)S(1)}, bf16[128,2304]{1,0:T(8,128)(2,1)S(1)}, u32[]{:S(2)}, u32[]{:S(2)}) collective-permute-start(bf16[128,2304]{1,0:T(8,128)(2,1)S(1)} %slice.26), channel_id=1, source_target_pairs={{96,0},{112,16},{0,32},{16,48},{32,64},{48,80},{64,96},{80,112},{9... | collective-permute-start | bytes 1769480 | tf_op jit(solution)/shard_map/ppermute | solution.py:57
  342.9 10.2 %collective-permute-start.7 = (bf16[1024,2304]{1,0:T(8,128)(2,1)S(1)}, bf16[1024,2304]{1,0:T(8,128)(2,1)S(1)}, u32[]{:S(2)}, u32[]{:S(2)}) collective-permute-start(bf16[1024,2304]{1,0:T(8,128)(2,1)S(1)} %get-tuple-element.4), channel_id=1, source_target_pairs={{128,0},{0,128},{129,1},{1,129},{130,2},{2,130},{131,3},{3,131},{1... | collective-permute-start | bytes 14155784 | tf_op jit(solution)/shard_map/ppermute | solution.py:59
  353.4 3.7 copy-start
